TPU v7x, 256 devices: a whole 4x4x8 slice. The times are simulated.
256 devices in a mesh: dp: 32 (over y, z), tensor: 8 (over x, core).
Axes of the slice: x: 4, y: 4, z: 8, core: 2. Of those that a mesh axis runs over, the one named last changes fastest.
Arguments:
- residual_in: bfloat16 [2048, 2048], P(('dp', 'tensor')), may hold values from -6 to 6
- attn_gain: float32 [2048], replicated, may hold values from 0.5 to 1.5
- query_weight: bfloat16 [2048, 4096], P(None, 'tensor'), may hold values from -0.125 to 0.125
- kv_weight: bfloat16 [2048, 1024], P(None, 'tensor'), may hold values from -0.125 to 0.125
- query_gain: float32 [128], replicated, may hold values from 0.25 to 1.75
- key_gain: float32 [128], replicated, may hold values from 0.25 to 1.75
- out_weight: bfloat16 [4096, 2048], P('tensor'), may hold values from -0.09375 to 0.09375
- moe_gain: float32 [2048], replicated, may hold values from 0.5 to 1.5
- gate_weight: bfloat16 [128, 2048, 768], P('dp', None, 'tensor'), may hold values from -0.1875 to 0.1875
- lift_weight: bfloat16 [128, 2048, 768], P('dp', None, 'tensor'), may hold values from -0.1875 to 0.1875
- down_weight: bfloat16 [128, 768, 2048], P('dp', 'tensor'), may hold values from -0.21875 to 0.21875
- routes: int32 [2048, 8], P('dp'), may hold values from 0 to 127, as said below
- route_weights: float32 [2048, 8], P('dp'), may hold values from 0.5 to 1
- prefix_cache: bfloat16 [64, 2048, 1024], P('dp', 'tensor'), may hold values from -250 to 250
- suffix_cache: bfloat16 [2048, 128, 1024], P('dp', 'tensor'), may hold values from -250 to 250
- prefix_len: int32 [64], P('dp'), may hold values from 1 to 2048, as said below
- suffix_len: int32 [2048], P('dp'), may hold values from 1 to 128, as said below
- request_group: int32 [2048], P('dp'), may hold values from 0 to 63, as said below
Outputs:
- layer_out: bfloat16 [2048, 2048], P(('dp', 'tensor'))
- new_cache_rows: bfloat16 [2048, 1024], P('dp', 'tensor')
Inputs may be any that keep to these rules, and one draw needn't show every extreme that they name: `routes`: each block of 64 rows (the requests of one index of dp) names 64 of the experts exactly 8 times each and no other expert; one expert is among them in every block. `request_group`: request r belongs to one of the groups (r // 64) * 2 to (r // 64) * 2 + 1. `prefix_len`: some shared prompt has all 2048 slots live. `suffix_len`: some request has all 128 suffix slots live.
All inputs are finite; a program needn't handle non-finite values.
Results may differ from a plain program's by a relative error of at most 0.02.
Values may be sent and summed in bfloat16 or wider, within the bound.
No kernel may reach another device: no remote copies, remote signals or barrier semaphores. Data moves between devices by JAX's collectives and lax.ppermute only.
A program may use at most 128 MiB of HBM per device.

v0:
```python
import math
import jax
import jax.numpy as jnp
from jax import lax
from jax.sharding import Mesh, PartitionSpec as P

EPSILON = 1e-06
THETA = 1000000.0
NEGATIVE = -1e30
TENSOR = ("tx", "tc")


def rms_scale(values, gain):
    mean_square = jnp.mean(values * values, axis=-1, keepdims=True)
    return values * lax.rsqrt(mean_square + EPSILON) * gain


def rotate(values, positions):
    half = values.shape[-1] // 2
    freqs = THETA ** (-jnp.arange(half).astype(jnp.float32) * 2.0 / values.shape[-1])
    angles = positions.astype(jnp.float32)[:, None] * freqs[None, :]
    angles = jnp.concatenate([angles, angles], axis=-1)
    cosine = jnp.cos(angles)[:, None, :]
    sine = jnp.sin(angles)[:, None, :]
    turned = jnp.concatenate([-values[..., half:], values[..., :half]], axis=-1)
    return values * cosine + turned * sine


def body(
    residual_in,
    attn_gain,
    query_weight,
    kv_weight,
    query_gain,
    key_gain,
    out_weight,
    moe_gain,
    gate_weight,
    lift_weight,
    down_weight,
    routes,
    route_weights,
    prefix_cache,
    suffix_cache,
    prefix_len,
    suffix_len,
    request_group,
):
    tensor_size = lax.axis_size(TENSOR)
    chip_rank = lax.axis_index("tx")
    core_rank = lax.axis_index("tc")
    chips = lax.axis_size("tx")
    tensor_rank = chip_rank * lax.axis_size("tc") + core_rank
    chunk_rank = core_rank * chips + chip_rank
    dp_rank = lax.axis_index("dp")
    owners = lax.axis_size("dp")
    head_dim = query_gain.shape[0]
    requests = routes.shape[0]
    model_width = residual_in.shape[1]
    query_cols = query_weight.shape[1]
    kv_cols = kv_weight.shape[1]
    heads_here = query_cols // head_dim
    heads_all = heads_here * tensor_size
    kv_heads_all = kv_cols * tensor_size // (2 * head_dim)
    per_group = heads_all // kv_heads_all
    groups_dev = prefix_cache.shape[0]
    pre_local = prefix_cache.shape[1]
    suf_local = suffix_cache.shape[1]
    residual_all = lax.all_gather(residual_in, TENSOR, axis=0, tiled=True)
    piece = rms_scale(residual_all.astype(jnp.float32), attn_gain).astype(jnp.bfloat16)
    projected = jnp.concatenate(
        [
            jnp.dot(piece, query_weight, preferred_element_type=jnp.float32),
            jnp.dot(piece, kv_weight, preferred_element_type=jnp.float32),
        ],
        axis=1,
    )
    query_raw = projected[:, :query_cols].reshape(requests, heads_here, head_dim)
    kv_raw = projected[:, query_cols:].reshape(requests, kv_cols // head_dim, head_dim)
    group_ids = dp_rank * groups_dev + jnp.arange(groups_dev)
    member = request_group[:, None] == group_ids[None, :]
    prefix_of = jnp.sum(jnp.where(member, prefix_len[None, :], 0), axis=1)
    positions = prefix_of + suffix_len
    queries = rotate(rms_scale(query_raw, query_gain), positions).astype(jnp.bfloat16)
    head_number = tensor_rank * (kv_cols // head_dim) + jnp.arange(kv_cols // head_dim)
    is_key = (head_number < kv_heads_all)[None, :, None]
    keyed = rotate(rms_scale(kv_raw, key_gain), positions)
    new_rows = jnp.where(is_key, keyed, kv_raw).astype(jnp.bfloat16).reshape(requests, kv_cols)
    joined = jnp.concatenate([queries.reshape(requests, query_cols), new_rows], axis=1)
    every_head = lax.all_gather(joined, TENSOR, axis=1, tiled=True).reshape(
        requests, tensor_size, query_cols + kv_cols
    )
    all_queries = every_head[:, :, :query_cols].reshape(requests, kv_heads_all, per_group, head_dim)
    all_kv = every_head[:, :, query_cols:]
    own_keys = all_kv[:, :kv_heads_all]
    own_values = all_kv[:, kv_heads_all:].astype(jnp.float32)
    scale = 1.0 / math.sqrt(head_dim)
    split_at = kv_heads_all * head_dim
    pre_keys = prefix_cache[:, :, :split_at].reshape(groups_dev, pre_local, kv_heads_all, head_dim)
    pre_values = prefix_cache[:, :, split_at:].reshape(
        groups_dev, pre_local, kv_heads_all, head_dim
    )
    suf_keys = suffix_cache[:, :, :split_at].reshape(requests, suf_local, kv_heads_all, head_dim)
    suf_values = suffix_cache[:, :, split_at:].reshape(requests, suf_local, kv_heads_all, head_dim)
    pre_scores = (
        jnp.einsum("rgqd,npgd->rgqnp", all_queries, pre_keys, preferred_element_type=jnp.float32)
        * scale
    )
    suf_scores = (
        jnp.einsum("rgqd,rsgd->rgqs", all_queries, suf_keys, preferred_element_type=jnp.float32)
        * scale
    )
    own_scores = (
        jnp.einsum("rgqd,rgd->rgq", all_queries, own_keys, preferred_element_type=jnp.float32)
        * scale
    )
    pre_slots = tensor_rank * pre_local + jnp.arange(pre_local)
    pre_valid = (member[:, :, None] & (pre_slots[None, None, :] < prefix_len[None, :, None]))[
        :, None, None, :, :
    ]
    suf_slots = tensor_rank * suf_local + jnp.arange(suf_local)
    suf_valid = (suf_slots[None, :] < suffix_len[:, None])[:, None, None, :]
    own_valid = tensor_rank == 0
    top_pre = jnp.max(jnp.where(pre_valid, pre_scores, NEGATIVE), axis=(3, 4))
    top_suf = jnp.max(jnp.where(suf_valid, suf_scores, NEGATIVE), axis=3)
    top_own = jnp.where(own_valid, own_scores, NEGATIVE)
    top_local = jnp.maximum(jnp.maximum(top_pre, top_suf), top_own)
    pre_weights = jnp.where(pre_valid, jnp.exp(pre_scores - top_local[..., None, None]), 0.0)
    suf_weights = jnp.where(suf_valid, jnp.exp(suf_scores - top_local[..., None]), 0.0)
    own_weights = jnp.where(own_valid, jnp.exp(own_scores - top_local), 0.0)
    total_local = jnp.sum(pre_weights, axis=(3, 4)) + jnp.sum(suf_weights, axis=3) + own_weights
    sums_local = jnp.einsum(
        "rgqnp,npgd->rgqd",
        pre_weights.astype(jnp.bfloat16),
        pre_values,
        preferred_element_type=jnp.float32,
    )
    sums_local = sums_local + jnp.einsum(
        "rgqs,rsgd->rgqd",
        suf_weights.astype(jnp.bfloat16),
        suf_values,
        preferred_element_type=jnp.float32,
    )
    own_low = own_weights.astype(jnp.bfloat16).astype(jnp.float32)
    sums_local = sums_local + own_low[..., None] * own_values[:, :, None, :]
    packed = jnp.concatenate(
        [
            sums_local.reshape(requests, heads_all, head_dim),
            top_local.reshape(requests, heads_all, 1),
            total_local.reshape(requests, heads_all, 1),
        ],
        axis=2,
    )
    packed = packed.reshape(requests, tensor_size, heads_here, head_dim + 2).transpose(1, 0, 2, 3)
    parts = lax.all_to_all(packed, TENSOR, 0, 0, tiled=True)
    part_sums = parts[..., :head_dim]
    part_top = parts[..., head_dim]
    part_total = parts[..., head_dim + 1]
    top_all = jnp.max(part_top, axis=0)
    factor = jnp.exp(part_top - top_all[None])
    total_mine = jnp.sum(part_total * factor, axis=0)
    sums_mine = jnp.sum(part_sums * factor[..., None], axis=0)
    mixed = sums_mine / total_mine[..., None]
    attn_heads = mixed.reshape(requests, query_cols).astype(jnp.bfloat16)
    attn_all = lax.psum(jnp.dot(attn_heads, out_weight, preferred_element_type=jnp.float32), TENSOR)
    middle_all = (residual_all.astype(jnp.float32) + attn_all).astype(jnp.bfloat16)
    tokens_here = residual_in.shape[0]
    middle = lax.dynamic_slice_in_dim(middle_all, tensor_rank * tokens_here, tokens_here, 0)
    moe_all = rms_scale(middle_all.astype(jnp.float32), moe_gain).astype(jnp.bfloat16)
    local_experts = gate_weight.shape[0]
    experts_all = local_experts * owners
    topk = routes.shape[1]
    capacity = 2 * requests * topk // experts_all
    flat_routes = routes.reshape(-1)
    onehot = (flat_routes[:, None] == jnp.arange(experts_all)[None, :]).astype(jnp.int32)
    running = jnp.cumsum(onehot, axis=0)
    slot_of = jnp.sum(onehot * running, axis=1) - 1
    code_of = (flat_routes * capacity + slot_of).reshape(requests, topk)
    code_span = jnp.arange(experts_all * capacity)
    placing = jnp.any(code_of[None, :, :] == code_span[:, None, None], axis=2).astype(jnp.bfloat16)
    share = route_weights / jnp.sum(route_weights, axis=1, keepdims=True)
    width_here = model_width // tensor_size
    cols_in = lax.dynamic_slice_in_dim(moe_all, chunk_rank * width_here, width_here, 1)
    placed = jnp.dot(placing, cols_in, preferred_element_type=jnp.float32)
    outgoing = placed.astype(jnp.bfloat16).reshape(owners, local_experts * capacity, width_here)
    arrived = lax.all_to_all(outgoing, "dp", split_axis=0, concat_axis=0, tiled=True)
    half_rows = lax.all_gather(arrived, "tx", axis=2, tiled=True)
    rows = lax.all_gather(half_rows, "tc", axis=2, tiled=True).reshape(
        owners, local_experts, capacity, model_width
    )
    gate_val = jnp.einsum("necd,edf->necf", rows, gate_weight, preferred_element_type=jnp.float32)
    lift_val = jnp.einsum("necd,edf->necf", rows, lift_weight, preferred_element_type=jnp.float32)
    hidden_units = (jax.nn.silu(gate_val) * lift_val).astype(jnp.bfloat16)
    partial_out = jnp.einsum(
        "necf,efd->necd", hidden_units, down_weight, preferred_element_type=jnp.float32
    ).astype(jnp.bfloat16)
    core_out = lax.psum_scatter(partial_out, "tc", scatter_dimension=3, tiled=True)
    summed_out = lax.psum_scatter(core_out, "tx", scatter_dimension=3, tiled=True)
    returned = lax.all_to_all(
        summed_out.reshape(owners, local_experts * capacity, width_here),
        "dp",
        split_axis=0,
        concat_axis=0,
        tiled=True,
    ).astype(jnp.float32)
    returned = returned.reshape(experts_all * capacity, width_here)
    picked_rows = returned[code_of]
    moe_cols = jnp.sum(share[:, :, None] * picked_rows, axis=1).astype(jnp.bfloat16)
    moe_chunks = lax.all_to_all(moe_cols, TENSOR, split_axis=0, concat_axis=1, tiled=True)
    moe_out = (
        moe_chunks.reshape(tokens_here, chips, tensor_size // chips, width_here)
        .transpose(0, 2, 1, 3)
        .reshape(tokens_here, model_width)
        .astype(jnp.float32)
    )
    layer_out = (middle.astype(jnp.float32) + moe_out).astype(jnp.bfloat16)
    return (layer_out, new_rows)


def solution(mesh):
    cores = mesh.devices.shape[1] // 2
    split_mesh = Mesh(mesh.devices.reshape(mesh.devices.shape[0], cores, 2), ("dp", "tx", "tc"))
    in_specs = (
        P(("dp", "tx", "tc"), None),
        P(),
        P(None, TENSOR),
        P(None, TENSOR),
        P(),
        P(),
        P(TENSOR, None),
        P(),
        P("dp", None, TENSOR),
        P("dp", None, TENSOR),
        P("dp", TENSOR, None),
        P("dp", None),
        P("dp", None),
        P("dp", TENSOR, None),
        P("dp", TENSOR, None),
        P("dp"),
        P("dp"),
        P("dp"),
    )
    out_specs = (P(("dp", "tx", "tc"), None), P("dp", TENSOR))
    return jax.shard_map(
        body, mesh=split_mesh, in_specs=in_specs, out_specs=out_specs, check_vma=False
    )
```

profile of v0, /device:TPU:32, one launch (start us, length us, event | category | flops | bytes accessed | tf_op | source)
XLA Modules:
  0.0 390.6 jit_solution(887518312369594651)
XLA Ops:
  7.3 13.5 %all_gather.12 = bf16[64,2048]{1,0:T(8,128)(2,1)S(1)} all-gather(bf16[8,2048]{1,0:T(8,128)(2,1)} %param.18), channel_id=1, replica_groups=mesh['dp'=32,'tx'=4,'tc'=2] {'tx','tc'}, dimensions={0}, use_global_device_ids=true | all-gather | bytes 294912 | tf_op jit(solution)/shard_map/all_gather | solution.py:69
  20.9 1.4 multiply_reduce_fusion.2
  23.2 2.1 fusion.80
  26.8 13.3 %all_gather.13 = bf16[64,5120]{1,0:T(8,128)(2,1)S(1)} all-gather(bf16[64,640]{1,0:T(8,128)(2,1)S(1)} %pad_maximum_fusion), channel_id=1, replica_groups=mesh['dp'=32,'tx'=4,'tc'=2] {'tx','tc'}, dimensions={1}, use_global_device_ids=true | all-gather | bytes 737280 | tf_op jit(solution)/shard_map/all_gather | solution.py:90
  42.0 2.1 fusion.107
  44.0 2.0 copy.308
  46.2 4.6 %fusion = (f32[64,4,8]{2,0,1:T(8,128)}, f32[4,64,8,2,256]{4,2,3,1,0:T(8,128)}) fusion(pred[64,2,256]{2,1,0:T(4,128)(4,1)S(1)} %broadcast_and_fusion, bf16[2,256,4,128,1]{1,3,2,0,4:T(8,128)(2,1)} %bitcast.194, bf16[64,4,8,128]{3,2,1,0:T(8,128)(2,1)S(1)} %reshape.329), kind=kOutput, calls=%fused_computation.3 | convolution fusion | flops 271579136 | bytes 5283840 | tf_op jit(solution)/shard_map/rgqd,npgd->rgqnp/dot_general | solution.py:106
  50.8 1.6 copy.258
  52.5 2.9 slice_bitcast_fusion
  55.4 2.4 select_reduce_fusion
  57.8 1.0 copy.259
  58.8 1.4 convert_convert_fusion
  61.0 1.0 copy.309
  62.0 4.4 %fusion.7 = f32[64,4,8]{2,0,1:T(8,128)} fusion(f32[4,64,8,2,256]{4,2,3,1,0:T(8,128)} %get-tuple-element.29, f32[64,4,8]{2,0,1:T(8,128)S(1)} %copy.260, pred[64,2,256]{2,1,0:T(4,128)(4,1)S(1)} %broadcast_and_fusion), kind=kLoop, calls=%fused_computation.11 | loop fusion | flops 4192256 | bytes 4243456 | tf_op jit(solution)/shard_map/reduce_sum | solution.py:131
  66.5 3.2 fusion.19
  69.7 1.5 copy.266
  71.2 1.6 fusion.53
  72.8 2.0 fusion.22
  75.7 1.0 copy.269
  76.7 0.8 add_add_fusion
  77.4 1.4 copy.272
  78.8 1.4 copy.271
  80.3 3.3 maximum_bitcast_fusion
  83.5 4.3 %all-to-all-start = ((f32[8,64,4,130]{3,1,2,0:T(8,128)}), f32[8,64,4,130]{3,1,2,0:T(8,128)}, u32[]{:S(2)}, u32[]{:S(2)}) async-start(f32[8,64,4,130]{3,1,2,0:T(8,128)} %maximum_bitcast_fusion), calls=%async_computation | async-start | bytes 4194304 | tf_op jit(solution)/shard_map/all_to_all | solution.py:155
  89.2 25.8 %all-to-all-done = f32[8,64,4,130]{3,1,2,0:T(8,128)} async-done(((f32[8,64,4,130]{3,1,2,0:T(8,128)}), f32[8,64,4,130]{3,1,2,0:T(8,128)}, u32[]{:S(2)}, u32[]{:S(2)}) %all-to-all-start) | async-done | bytes 1064992 | tf_op jit(solution)/shard_map/all_to_all | solution.py:155
  115.0 3.0 fusion.106
  118.1 1.6 copy.311
  120.1 1.6 fusion.51
  121.7 1.3 fusion.82
  123.2 0.8 dynamic-slice
  124.7 65.4 %all-reduce.2.cloned.1.call-done = f32[64,2048]{1,0:T(8,128)} async-done(((f32[64,2048]{1,0:T(8,128)}), f32[64,2048]{1,0:T(8,128)}) %all-reduce.2.cloned.1.call-update) | async-done | bytes 524304 | tf_op jit(solution)/shard_map/psum | solution.py:165
  190.1 1.2 multiply_reduce_fusion
  192.4 25.5 %all_to_all.25 = bf16[32,32,256]{2,1,0:T(8,128)(2,1)} all-to-all(bf16[32,32,256]{2,1,0:T(8,128)(2,1)S(1)} %bitcast.193), channel_id=1, replica_groups=mesh['dp'=32,'tx'=4,'tc'=2] {'dp'}, dimensions={0} | all-to-all | bytes 1048576 | tf_op jit(solution)/shard_map/all_to_all | solution.py:186
  218.0 33.2 %all-gather.3.cloned.1.call-done = bf16[32,32,1024]{2,1,0:T(8,128)(2,1)} async-done(((bf16[32,32,256]{2,1,0:T(8,128)(2,1)}), bf16[32,32,1024]{2,1,0:T(8,128)(2,1)}) %all-gather.3.cloned.1.call-update) | async-done | bytes 2097168 | tf_op jit(solution)/shard_map/all_gather | solution.py:187
  251.3 21.8 %all-gather.5.cloned.1.call-done = bf16[32,32,2048]{2,1,0:T(8,128)(2,1)} async-done(((bf16[32,32,1024]{2,1,0:T(8,128)(2,1)}), bf16[32,32,2048]{2,1,0:T(8,128)(2,1)}) %all-gather.5.cloned.1.call-update) | async-done | bytes 4194320 | tf_op jit(solution)/shard_map/all_gather | solution.py:188
  273.0 3.9 %fusion.23 = f32[32,4,8,96]{3,2,0,1:T(8,128)S(1)} fusion(bf16[4,2048,96]{1,2,0:T(8,128)(2,1)} %param.26, bf16[32,32,2048]{2,1,0:T(8,128)(2,1)} %all-gather.5.cloned.1.call-done), kind=kOutput, calls=%fused_computation.29 | convolution fusion | flops 402653184 | bytes 6160384 | tf_op jit(solution)/shard_map/necd,edf->necf/dot_general | solution.py:191
  276.9 7.4 %convert_bitcast_fusion = bf16[32,4,8,2048]{3,2,0,1:T(8,128)(2,1)} fusion(bf16[4,96,2048]{2,1,0:T(8,128)(2,1)} %param.28, bf16[4,2048,96]{1,2,0:T(8,128)(2,1)} %param.27, f32[32,4,8,96]{3,2,0,1:T(8,128)S(1)} %fusion.23, bf16[32,32,2048]{2,1,0:T(8,128)(2,1)} %all-gather.5.cloned.1.call-done), kind=kOutput, calls=%fused_computation.6 | convolution fusion | flops 807993344 | bytes 11927552 | tf_op jit(solution)/shard_map/necf,efd->necd/dot_general | solution.py:194
  284.4 18.7 %reduce-scatter.3.cloned.1.call-done = bf16[32,4,8,1024]{3,2,0,1:T(8,128)(2,1)} async-done(((bf16[32,4,8,2048]{3,2,0,1:T(8,128)(2,1)}), bf16[32,4,8,1024]{3,2,0,1:T(8,128)(2,1)}) %reduce-scatter.3.cloned.1.call-update) | async-done | bytes 2097168 | tf_op jit(solution)/shard_map/reduce_scatter | solution.py:197
  303.1 35.9 %reduce-scatter.5.cloned.1.call-done = bf16[32,4,8,256]{3,2,0,1:T(8,128)(2,1)} async-done(((bf16[32,4,8,1024]{3,2,0,1:T(8,128)(2,1)}), bf16[32,4,8,256]{3,2,0,1:T(8,128)(2,1)}) %reduce-scatter.5.cloned.1.call-update) | async-done | bytes 524304 | tf_op jit(solution)/shard_map/reduce_scatter | solution.py:198
  339.1 1.9 copy.369
  341.0 10.1 %all-to-all-start.2 = ((bf16[32,32,256]{2,1,0:T(8,128)(2,1)}), bf16[32,32,256]{2,1,0:T(8,128)(2,1)}, u32[]{:S(2)}, u32[]{:S(2)}) async-start(bf16[32,32,256]{2,1,0:T(8,128)(2,1)} %bitcast.185), calls=%async_computation.4 | async-start | bytes 1048576 | tf_op jit(solution)/shard_map/all_to_all | solution.py:199
  351.4 17.3 %all-to-all-done.2 = bf16[32,32,256]{2,1,0:T(8,128)(2,1)} async-done(((bf16[32,32,256]{2,1,0:T(8,128)(2,1)}), bf16[32,32,256]{2,1,0:T(8,128)(2,1)}, u32[]{:S(2)}, u32[]{:S(2)}) %all-to-all-start.2) | async-done | bytes 524320 | tf_op jit(solution)/shard_map/all_to_all | solution.py:199
  368.7 1.1 bitcast_convert_fusion
  369.8 2.2 gather_fusion
  372.1 1.9 fusion.58
  373.9 3.3 all-to-all-start.3
  377.3 5.4 %all-to-all-done.3 = bf16[8,8,256]{2,1,0:T(8,128)(2,1)S(1)} async-done(((bf16[8,8,256]{2,1,0:T(8,128)(2,1)}), bf16[8,8,256]{2,1,0:T(8,128)(2,1)S(1)}, u32[]{:S(2)}, u32[]{:S(2)}) %all-to-all-start.3) | async-done | bytes 32800 | tf_op jit(solution)/shard_map/all_to_all | solution.py:209
  382.7 1.4 add_convert_fusion
  (116 shorter events, 10.1 us)
Async XLA Ops:
  7.2 114.5 %copy-start = (bf16[512,2048]{1,0:T(8,128)(2,1)S(1)}, bf16[512,2048]{1,0:T(8,128)(2,1)}, u32[]{:S(2)}) copy-start(bf16[512,2048]{1,0:T(8,128)(2,1)} %param.24) | copy-start | bytes 6291460
  7.2 19.0 %copy-start.9 = (f32[128]{0:T(128)S(1)}, f32[128]{0:T(128)}, u32[]{:S(2)}) copy-start(f32[128]{0:T(128)} %param.23) | copy-start | bytes 1540
  7.2 18.4 %copy-start.10 = (f32[128]{0:T(128)S(1)}, f32[128]{0:T(128)}, u32[]{:S(2)}) copy-start(f32[128]{0:T(128)} %param.22) | copy-start | bytes 1540
  7.2 18.7 %copy-start.12 = (s32[2]{0:T(128)S(1)}, s32[2]{0:T(128)}, u32[]{:S(2)}) copy-start(s32[2]{0:T(128)} %param.33) | copy-start | bytes 28
  7.2 18.7 %copy-start.11 = (s32[64]{0:T(128)S(1)}, s32[64]{0:T(128)}, u32[]{:S(2)}) copy-start(s32[64]{0:T(128)} %param.35) | copy-start | bytes 772
  7.2 18.9 %copy-start.15 = (s32[64]{0:T(128)S(1)}, s32[64]{0:T(128)}, u32[]{:S(2)}) copy-start(s32[64]{0:T(128)} %param.34) | copy-start | bytes 772
  23.2 3.0 copy-start.13
  26.2 14.1 %copy-start.14 = (s32[2]{0:T(128)S(1)}, s32[2]{0:T(128)}, u32[]{:S(2)}) copy-start(s32[2]{0:T(128)} %copy-done.13) | copy-start | bytes 28
  26.4 13.8 %copy-start.6 = (bf16[64,128]{1,0:T(8,128)(2,1)}, bf16[64,128]{1,0:T(8,128)(2,1)S(1)}, u32[]{:S(2)}) copy-start(bf16[64,128]{1,0:T(8,128)(2,1)S(1)} %get-tuple-element.22) | copy-start | bytes 49156
  41.9 10.5 %copy-start.16 = (s32[64]{0:T(128)S(1)}, s32[64]{0:T(128)}, u32[]{:S(2)}) copy-start(s32[64]{0:T(128)} %param.34) | copy-start | bytes 772
  52.5 5.3 %copy-start.5 = (pred[64,16]{1,0:T(8,128)(4,1)}, pred[64,16]{1,0:T(8,128)(4,1)S(1)}, u32[]{:S(2)}) copy-start(pred[64,16]{1,0:T(8,128)(4,1)S(1)} %broadcast_compare_fusion) | copy-start | bytes 3076
  60.2 1.8 copy-start.4
  62.0 4.4 %copy-start.1 = (f32[4,64,8,2,256]{4,2,3,1,0:T(8,128)S(1)}, f32[4,64,8,2,256]{4,2,3,1,0:T(8,128)}, u32[]{:S(2)}) copy-start(f32[4,64,8,2,256]{4,2,3,1,0:T(8,128)} %get-tuple-element.29) | copy-start | bytes 12582916
  66.5 4.7 %copy-start.2 = (f32[64,4,8,16]{3,2,1,0:T(8,128)S(1)}, f32[64,4,8,16]{3,2,1,0:T(8,128)}, u32[]{:S(2)}) copy-start(f32[64,4,8,16]{3,2,1,0:T(8,128)} %get-tuple-element.31) | copy-start | bytes 393220
  80.3 7.8 %copy-start.8 = (s32[64,8]{0,1:T(8,128)S(1)}, s32[64,8]{0,1:T(8,128)}, u32[]{:S(2)}) copy-start(s32[64,8]{0,1:T(8,128)} %param.29) | copy-start | bytes 6148
  83.5 31.5 %all-to-all-start = ((f32[8,64,4,130]{3,1,2,0:T(8,128)}), f32[8,64,4,130]{3,1,2,0:T(8,128)}, u32[]{:S(2)}, u32[]{:S(2)}) async-start(f32[8,64,4,130]{3,1,2,0:T(8,128)} %maximum_bitcast_fusion), calls=%async_computation | async-start | bytes 4194304 | tf_op jit(solution)/shard_map/all_to_all | solution.py:155
  87.9 102.2 %all-reduce.2.cloned.1.call-start = ((), (), s32[]{:S(2)}) async-start(), calls=%async_computation.6 | async-start | bytes 1048576 | tf_op jit(solution)/shard_map/psum | solution.py:165
  123.1 128.1 %all-gather.3.cloned.1.call-start = ((), (), s32[]{:S(2)}) async-start(), calls=%async_computation.7 | async-start | bytes 2621440 | tf_op jit(solution)/shard_map/all_gather | solution.py:187
  191.3 0.7 copy-start.3
  218.0 55.0 %all-gather.5.cloned.1.call-start = ((), (), s32[]{:S(2)}) async-start(), calls=%async_computation.8 | async-start | bytes 6291456 | tf_op jit(solution)/shard_map/all_gather | solution.py:188
  251.2 51.9 %reduce-scatter.3.cloned.1.call-start = ((), (), s32[]{:S(2)}) async-start(), calls=%async_computation.9 | async-start | bytes 6291456 | tf_op jit(solution)/shard_map/reduce_scatter | solution.py:197
  284.3 67.0 %copy-start.7 = (f32[64,8]{0,1:T(8,128)S(1)}, f32[64,8]{0,1:T(8,128)}, u32[]{:S(2)}) copy-start(f32[64,8]{0,1:T(8,128)} %param.30) | copy-start | bytes 6148
  284.4 54.7 %reduce-scatter.5.cloned.1.call-start = ((), (), s32[]{:S(2)}) async-start(), calls=%async_computation.10 | async-start | bytes 2621440 | tf_op jit(solution)/shard_map/reduce_scatter | solution.py:198
  341.0 27.7 %all-to-all-start.2 = ((bf16[32,32,256]{2,1,0:T(8,128)(2,1)}), bf16[32,32,256]{2,1,0:T(8,128)(2,1)}, u32[]{:S(2)}, u32[]{:S(2)}) async-start(bf16[32,32,256]{2,1,0:T(8,128)(2,1)} %bitcast.185), calls=%async_computation.4 | async-start | bytes 1048576 | tf_op jit(solution)/shard_map/all_to_all | solution.py:199
  373.9 8.7 %all-to-all-start.3 = ((bf16[8,8,256]{2,1,0:T(8,128)(2,1)}), bf16[8,8,256]{2,1,0:T(8,128)(2,1)S(1)}, u32[]{:S(2)}, u32[]{:S(2)}) async-start(bf16[8,8,256]{2,1,0:T(8,128)(2,1)} %bitcast.163), calls=%async_computation.5 | async-start | bytes 65536 | tf_op jit(solution)/shard_map/all_to_all | solution.py:209
Sparse Core Ops, SparseCore 0:
  123.2 66.8 all-reduce.1
  218.1 33.0 all-gather.2
  253.0 19.9 all-gather.4
  284.5 18.5 reduce-scatter.2
  305.5 33.5 reduce-scatter.4
where the time goes:
time: 392 us; the launch traced here: 391 us
  waiting for transfers between devices  224 us (57%)
  blocking collectives  52.4 us (13%)
  matrix products  29.2 us (7%)
  local copies, waits for them, and re-layouts  27.5 us (7%)
  other arithmetic  25.3 us (6%)
  starting transfers between devices  18.2 us (5%)
  between operations  14.4 us (4%)
    psum x1, waiting for transfers between devices, body(): lax.psum(jnp.dot(attn_heads, out_weight, preferred_element_type=jnp.float...  65.4 us
    reduce_scatter x1, waiting for transfers between devices, body(): lax.psum_scatter(core_out, 'tx', scatter_dimension=3, tiled=True)  35.9 us
    all_gather x1, waiting for transfers between devices, body(): half_rows = lax.all_gather(arrived, 'tx', axis=2, tiled=True)  33.2 us
    all_to_all x1, waiting for transfers between devices, body(): parts = lax.all_to_all(packed, TENSOR, 0, 0, tiled=True)  25.8 us
    all_to_all x1, blocking collectives, body(): lax.all_to_all(outgoing, 'dp', split_axis=0, concat_axis=0, tiled=True)  25.5 us
    all_gather x1, waiting for transfers between devices, body(): lax.all_gather(half_rows, 'tc', axis=2, tiled=True)  21.8 us
    reduce_scatter x1, waiting for transfers between devices, body(): lax.psum_scatter(partial_out, 'tc', scatter_dimension=3, tiled=True)  18.7 us
    all_to_all x1, waiting for transfers between devices, body(): lax.all_to_all(summed_out.reshape(owners, local_experts * capacity, width...  17.3 us
  transfers between devices with their start and end apart: 8, of which 8 were waited for; matrix products, arithmetic and copies ran while one was open for 1% of the time, Pallas kernels for 0%

commit v1 on v0

--- a/solution.py
+++ b/solution.py
@@ -162,7 +162,10 @@
     sums_mine = jnp.sum(part_sums * factor[..., None], axis=0)
     mixed = sums_mine / total_mine[..., None]
     attn_heads = mixed.reshape(requests, query_cols).astype(jnp.bfloat16)
-    attn_all = lax.psum(jnp.dot(attn_heads, out_weight, preferred_element_type=jnp.float32), TENSOR)
+    attn_all = jnp.sum(
+        lax.all_gather(jnp.dot(attn_heads, out_weight, preferred_element_type=jnp.float32), TENSOR),
+        0,
+    )
     middle_all = (residual_all.astype(jnp.float32) + attn_all).astype(jnp.bfloat16)
     tokens_here = residual_in.shape[0]
     middle = lax.dynamic_slice_in_dim(middle_all, tensor_rank * tokens_here, tokens_here, 0)

time: 392 us -> 359 us (0.916)
  waiting for transfers between devices: 224 us -> 163 us
  blocking collectives: 52.4 us -> 85.6 us
  starting transfers between devices: 18.2 us -> 13.7 us
    psum x1 -> x0, waiting for transfers between devices: 65.4 us -> none  [body(): lax.psum(jnp.dot(attn_heads, out_weight, preferred_element_type=jnp.float...]
    all_gather x0 -> x1, waiting for transfers between devices: none -> 32.7 us  [body(): lax.all_gather(jnp.dot(attn_heads, out_weight, preferred_element_type=jnp...]
    all_to_all x0 -> x1, blocking collectives: none -> 30.7 us  [body(): parts = lax.all_to_all(packed, TENSOR, 0, 0, tiled=True)]
    all_to_all x1 -> x0, waiting for transfers between devices: 25.8 us -> none  [body(): parts = lax.all_to_all(packed, TENSOR, 0, 0, tiled=True)]
    all_to_all x1 -> x0, starting transfers between devices: 4.34 us -> none  [body(): parts = lax.all_to_all(packed, TENSOR, 0, 0, tiled=True)]
    unnamed x42 -> x44, local copies, waits for them, and re-layouts: 8.87 us -> 9.58 us
  transfers between devices with their start and end apart: 8 -> 7, of which waited for: 8 -> 7; matrix products, arithmetic and copies ran while one was open for 1% -> 1% of each run, Pallas kernels for 0% -> 0%
where the time goes in v1:
time: 359 us; the launch traced here: 358 us
  waiting for transfers between devices  163 us (45%)
  blocking collectives  85.6 us (24%)
  matrix products  29.2 us (8%)
  local copies, waits for them, and re-layouts  28.3 us (8%)
  other arithmetic  23.9 us (7%)
  between operations  14.4 us (4%)
  starting transfers between devices  13.7 us (4%)
    reduce_scatter x1, waiting for transfers between devices, body(): lax.psum_scatter(core_out, 'tx', scatter_dimension=3, tiled=True)  35.9 us
    all_gather x1, waiting for transfers between devices, body(): lax.all_gather(jnp.dot(attn_heads, out_weight, preferred_element_type=jnp...  32.7 us
    all_gather x1, waiting for transfers between devices, body(): half_rows = lax.all_gather(arrived, 'tx', axis=2, tiled=True)  31.3 us
    all_to_all x1, blocking collectives, body(): parts = lax.all_to_all(packed, TENSOR, 0, 0, tiled=True)  30.7 us
    all_to_all x1, blocking collectives, body(): lax.all_to_all(outgoing, 'dp', split_axis=0, concat_axis=0, tiled=True)  28 us
    all_gather x1, waiting for transfers between devices, body(): lax.all_gather(half_rows, 'tc', axis=2, tiled=True)  21.8 us
    reduce_scatter x1, waiting for transfers between devices, body(): lax.psum_scatter(partial_out, 'tc', scatter_dimension=3, tiled=True)  18.7 us
    all_to_all x1, waiting for transfers between devices, body(): lax.all_to_all(summed_out.reshape(owners, local_experts * capacity, width...  17.3 us
  transfers between devices with their start and end apart: 7, of which 7 were waited for; matrix products, arithmetic and copies ran while one was open for 1% of the time, Pallas kernels for 0%

profile of v1, /device:TPU:32, one launch (start us, length us, event | category | flops | bytes accessed | tf_op | source)
XLA Modules:
  0.0 358.2 jit_solution(6526163685849980737)
XLA Ops:
  7.3 13.5 %all_gather.18 = bf16[64,2048]{1,0:T(8,128)(2,1)S(1)} all-gather(bf16[8,2048]{1,0:T(8,128)(2,1)} %param.18), channel_id=1, replica_groups=mesh['dp'=32,'tx'=4,'tc'=2] {'tx','tc'}, dimensions={0}, use_global_device_ids=true | all-gather | bytes 294912 | tf_op jit(solution)/shard_map/all_gather | solution.py:69
  21.0 1.4 multiply_reduce_fusion.2
  23.3 2.1 fusion.80
  26.9 13.3 %all_gather.19 = bf16[64,5120]{1,0:T(8,128)(2,1)S(1)} all-gather(bf16[64,640]{1,0:T(8,128)(2,1)S(1)} %pad_maximum_fusion), channel_id=1, replica_groups=mesh['dp'=32,'tx'=4,'tc'=2] {'tx','tc'}, dimensions={1}, use_global_device_ids=true | all-gather | bytes 737280 | tf_op jit(solution)/shard_map/all_gather | solution.py:90
  42.0 2.1 fusion.107
  44.1 2.0 copy.307
  46.3 4.6 %fusion = (f32[64,4,8]{2,0,1:T(8,128)}, f32[4,64,8,2,256]{4,2,3,1,0:T(8,128)}) fusion(pred[64,2,256]{2,1,0:T(4,128)(4,1)S(1)} %broadcast_and_fusion, bf16[2,256,4,128,1]{1,3,2,0,4:T(8,128)(2,1)} %bitcast.195, bf16[64,4,8,128]{3,2,1,0:T(8,128)(2,1)S(1)} %reshape.329), kind=kOutput, calls=%fused_computation.3 | convolution fusion | flops 271579136 | bytes 5283840 | tf_op jit(solution)/shard_map/rgqd,npgd->rgqnp/dot_general | solution.py:106
  50.9 1.6 copy.257
  52.6 2.9 slice_bitcast_fusion
  55.5 2.4 select_reduce_fusion
  57.9 1.0 copy.258
  58.8 1.4 convert_convert_fusion
  61.1 1.0 copy.308
  62.1 4.4 %fusion.7 = f32[64,4,8]{2,0,1:T(8,128)} fusion(f32[4,64,8,2,256]{4,2,3,1,0:T(8,128)} %get-tuple-element.29, f32[64,4,8]{2,0,1:T(8,128)S(1)} %copy.259, pred[64,2,256]{2,1,0:T(4,128)(4,1)S(1)} %broadcast_and_fusion), kind=kLoop, calls=%fused_computation.11 | loop fusion | flops 4192256 | bytes 4243456 | tf_op jit(solution)/shard_map/reduce_sum | solution.py:131
  66.5 3.2 fusion.19
  69.7 1.5 copy.265
  71.2 1.6 fusion.53
  72.8 2.0 fusion.22
  75.7 1.0 copy.268
  76.7 0.8 add_add_fusion
  77.5 1.4 copy.271
  78.9 1.4 copy.270
  80.3 1.9 maximum_bitcast_fusion
  82.3 30.7 %all_to_all.25 = f32[8,64,4,130]{3,1,2,0:T(8,128)S(1)} all-to-all(f32[8,64,4,130]{3,1,2,0:T(8,128)S(1)} %maximum_bitcast_fusion), channel_id=1, replica_groups=mesh['dp'=32,'tx'=4,'tc'=2] {'tx','tc'}, dimensions={0} | all-to-all | bytes 2129920 | tf_op jit(solution)/shard_map/all_to_all | solution.py:155
  112.9 1.3 copy-done.2
  114.3 1.4 fusion.106
  115.7 1.6 copy.310
  117.8 1.6 fusion.51
  119.3 1.3 fusion.82
  122.0 0.8 dynamic-slice
  123.4 32.7 %all-gather.9.cloned.1.call-done = f32[512,2048]{1,0:T(8,128)} async-done(((f32[64,2048]{1,0:T(8,128)}), f32[512,2048]{1,0:T(8,128)}) %all-gather.9.cloned.1.call-update) | async-done | bytes 4194320 | tf_op jit(solution)/shard_map/all_gather | solution.py:166
  156.2 2.5 reduce_sum.125
  159.3 28.0 %all_to_all.26 = bf16[32,32,256]{2,1,0:T(8,128)(2,1)} all-to-all(bf16[32,32,256]{2,1,0:T(8,128)(2,1)S(1)} %bitcast.194), channel_id=1, replica_groups=mesh['dp'=32,'tx'=4,'tc'=2] {'dp'}, dimensions={0} | all-to-all | bytes 1048576 | tf_op jit(solution)/shard_map/all_to_all | solution.py:189
  187.4 31.3 %all-gather.5.cloned.1.call-done = bf16[32,32,1024]{2,1,0:T(8,128)(2,1)} async-done(((bf16[32,32,256]{2,1,0:T(8,128)(2,1)}), bf16[32,32,1024]{2,1,0:T(8,128)(2,1)}) %all-gather.5.cloned.1.call-update) | async-done | bytes 2097168 | tf_op jit(solution)/shard_map/all_gather | solution.py:190
  218.8 21.8 %all-gather.7.cloned.1.call-done = bf16[32,32,2048]{2,1,0:T(8,128)(2,1)} async-done(((bf16[32,32,1024]{2,1,0:T(8,128)(2,1)}), bf16[32,32,2048]{2,1,0:T(8,128)(2,1)}) %all-gather.7.cloned.1.call-update) | async-done | bytes 4194320 | tf_op jit(solution)/shard_map/all_gather | solution.py:191
  240.5 3.9 %fusion.23 = f32[32,4,8,96]{3,2,0,1:T(8,128)S(1)} fusion(bf16[4,2048,96]{1,2,0:T(8,128)(2,1)} %param.26, bf16[32,32,2048]{2,1,0:T(8,128)(2,1)} %all-gather.7.cloned.1.call-done), kind=kOutput, calls=%fused_computation.29 | convolution fusion | flops 402653184 | bytes 6160384 | tf_op jit(solution)/shard_map/necd,edf->necf/dot_general | solution.py:194
  244.5 7.4 %convert_bitcast_fusion = bf16[32,4,8,2048]{3,2,0,1:T(8,128)(2,1)} fusion(bf16[4,96,2048]{2,1,0:T(8,128)(2,1)} %param.28, bf16[4,2048,96]{1,2,0:T(8,128)(2,1)} %param.27, f32[32,4,8,96]{3,2,0,1:T(8,128)S(1)} %fusion.23, bf16[32,32,2048]{2,1,0:T(8,128)(2,1)} %all-gather.7.cloned.1.call-done), kind=kOutput, calls=%fused_computation.6 | convolution fusion | flops 807993344 | bytes 11927552 | tf_op jit(solution)/shard_map/necf,efd->necd/dot_general | solution.py:197
  251.9 18.7 %reduce-scatter.3.cloned.1.call-done = bf16[32,4,8,1024]{3,2,0,1:T(8,128)(2,1)} async-done(((bf16[32,4,8,2048]{3,2,0,1:T(8,128)(2,1)}), bf16[32,4,8,1024]{3,2,0,1:T(8,128)(2,1)}) %reduce-scatter.3.cloned.1.call-update) | async-done | bytes 2097168 | tf_op jit(solution)/shard_map/reduce_scatter | solution.py:200
  270.7 35.9 %reduce-scatter.5.cloned.1.call-done = bf16[32,4,8,256]{3,2,0,1:T(8,128)(2,1)} async-done(((bf16[32,4,8,1024]{3,2,0,1:T(8,128)(2,1)}), bf16[32,4,8,256]{3,2,0,1:T(8,128)(2,1)}) %reduce-scatter.5.cloned.1.call-update) | async-done | bytes 524304 | tf_op jit(solution)/shard_map/reduce_scatter | solution.py:201
  306.6 1.9 copy.368
  308.5 10.1 %all-to-all-start.2 = ((bf16[32,32,256]{2,1,0:T(8,128)(2,1)}), bf16[32,32,256]{2,1,0:T(8,128)(2,1)}, u32[]{:S(2)}, u32[]{:S(2)}) async-start(bf16[32,32,256]{2,1,0:T(8,128)(2,1)} %bitcast.185), calls=%async_computation.4 | async-start | bytes 1048576 | tf_op jit(solution)/shard_map/all_to_all | solution.py:202
  319.0 17.3 %all-to-all-done.2 = bf16[32,32,256]{2,1,0:T(8,128)(2,1)} async-done(((bf16[32,32,256]{2,1,0:T(8,128)(2,1)}), bf16[32,32,256]{2,1,0:T(8,128)(2,1)}, u32[]{:S(2)}, u32[]{:S(2)}) %all-to-all-start.2) | async-done | bytes 524320 | tf_op jit(solution)/shard_map/all_to_all | solution.py:202
  336.3 1.1 bitcast_convert_fusion
  337.4 2.2 gather_fusion
  339.6 1.9 fusion.58
  341.5 3.3 all-to-all-start.3
  344.8 5.4 %all-to-all-done.3 = bf16[8,8,256]{2,1,0:T(8,128)(2,1)S(1)} async-done(((bf16[8,8,256]{2,1,0:T(8,128)(2,1)}), bf16[8,8,256]{2,1,0:T(8,128)(2,1)S(1)}, u32[]{:S(2)}, u32[]{:S(2)}) %all-to-all-start.3) | async-done | bytes 32800 | tf_op jit(solution)/shard_map/all_to_all | solution.py:212
  350.3 1.4 add_convert_fusion
  (119 shorter events, 9.6 us)
Async XLA Ops:
  7.2 112.2 %copy-start = (bf16[512,2048]{1,0:T(8,128)(2,1)S(1)}, bf16[512,2048]{1,0:T(8,128)(2,1)}, u32[]{:S(2)}) copy-start(bf16[512,2048]{1,0:T(8,128)(2,1)} %param.24) | copy-start | bytes 6291460
  7.2 19.1 %copy-start.10 = (f32[128]{0:T(128)S(1)}, f32[128]{0:T(128)}, u32[]{:S(2)}) copy-start(f32[128]{0:T(128)} %param.23) | copy-start | bytes 1540
  7.2 18.5 %copy-start.11 = (f32[128]{0:T(128)S(1)}, f32[128]{0:T(128)}, u32[]{:S(2)}) copy-start(f32[128]{0:T(128)} %param.22) | copy-start | bytes 1540
  7.2 18.7 %copy-start.13 = (s32[2]{0:T(128)S(1)}, s32[2]{0:T(128)}, u32[]{:S(2)}) copy-start(s32[2]{0:T(128)} %param.33) | copy-start | bytes 28
  7.2 18.7 %copy-start.12 = (s32[64]{0:T(128)S(1)}, s32[64]{0:T(128)}, u32[]{:S(2)}) copy-start(s32[64]{0:T(128)} %param.35) | copy-start | bytes 772
  7.2 18.9 %copy-start.16 = (s32[64]{0:T(128)S(1)}, s32[64]{0:T(128)}, u32[]{:S(2)}) copy-start(s32[64]{0:T(128)} %param.34) | copy-start | bytes 772
  7.2 148.9 %all-gather.9.cloned.1.call-start = ((), (), s32[]{:S(2)}) async-start(), calls=%async_computation.10 | async-start | bytes 4718592 | tf_op jit(solution)/shard_map/all_gather | solution.py:166
  23.3 3.0 copy-start.14
  26.3 14.1 %copy-start.15 = (s32[2]{0:T(128)S(1)}, s32[2]{0:T(128)}, u32[]{:S(2)}) copy-start(s32[2]{0:T(128)} %copy-done.14) | copy-start | bytes 28
  26.5 13.8 %copy-start.7 = (bf16[64,128]{1,0:T(8,128)(2,1)}, bf16[64,128]{1,0:T(8,128)(2,1)S(1)}, u32[]{:S(2)}) copy-start(bf16[64,128]{1,0:T(8,128)(2,1)S(1)} %get-tuple-element.22) | copy-start | bytes 49156
  42.0 10.5 %copy-start.17 = (s32[64]{0:T(128)S(1)}, s32[64]{0:T(128)}, u32[]{:S(2)}) copy-start(s32[64]{0:T(128)} %param.34) | copy-start | bytes 772
  52.5 5.3 %copy-start.6 = (pred[64,16]{1,0:T(8,128)(4,1)}, pred[64,16]{1,0:T(8,128)(4,1)S(1)}, u32[]{:S(2)}) copy-start(pred[64,16]{1,0:T(8,128)(4,1)S(1)} %broadcast_compare_fusion) | copy-start | bytes 3076
  60.3 1.8 copy-start.5
  62.1 4.4 %copy-start.1 = (f32[4,64,8,2,256]{4,2,3,1,0:T(8,128)S(1)}, f32[4,64,8,2,256]{4,2,3,1,0:T(8,128)}, u32[]{:S(2)}) copy-start(f32[4,64,8,2,256]{4,2,3,1,0:T(8,128)} %get-tuple-element.29) | copy-start | bytes 12582916
  66.5 4.7 %copy-start.3 = (f32[64,4,8,16]{3,2,1,0:T(8,128)S(1)}, f32[64,4,8,16]{3,2,1,0:T(8,128)}, u32[]{:S(2)}) copy-start(f32[64,4,8,16]{3,2,1,0:T(8,128)} %get-tuple-element.31) | copy-start | bytes 393220
  112.9 1.4 copy-start.2
  115.7 5.0 %copy-start.9 = (s32[64,8]{0,1:T(8,128)S(1)}, s32[64,8]{0,1:T(8,128)}, u32[]{:S(2)}) copy-start(s32[64,8]{0,1:T(8,128)} %param.29) | copy-start | bytes 6148
  120.7 98.0 %all-gather.5.cloned.1.call-start = ((), (), s32[]{:S(2)}) async-start(), calls=%async_computation.6 | async-start | bytes 2621440 | tf_op jit(solution)/shard_map/all_gather | solution.py:190
  158.8 85.6 %copy-start.4 = (bf16[64,2048]{1,0:T(8,128)(2,1)}, bf16[64,2048]{1,0:T(8,128)(2,1)S(1)}, u32[]{:S(2)}) copy-start(bf16[64,2048]{1,0:T(8,128)(2,1)S(1)} %get-tuple-element.5) | copy-start | bytes 786436
  187.3 53.2 %all-gather.7.cloned.1.call-start = ((), (), s32[]{:S(2)}) async-start(), calls=%async_computation.7 | async-start | bytes 6291456 | tf_op jit(solution)/shard_map/all_gather | solution.py:191
  218.7 52.0 %reduce-scatter.3.cloned.1.call-start = ((), (), s32[]{:S(2)}) async-start(), calls=%async_computation.8 | async-start | bytes 6291456 | tf_op jit(solution)/shard_map/reduce_scatter | solution.py:200
  251.9 67.0 %copy-start.8 = (f32[64,8]{0,1:T(8,128)S(1)}, f32[64,8]{0,1:T(8,128)}, u32[]{:S(2)}) copy-start(f32[64,8]{0,1:T(8,128)} %param.30) | copy-start | bytes 6148
  251.9 54.7 %reduce-scatter.5.cloned.1.call-start = ((), (), s32[]{:S(2)}) async-start(), calls=%async_computation.9 | async-start | bytes 2621440 | tf_op jit(solution)/shard_map/reduce_scatter | solution.py:201
  308.5 27.7 %all-to-all-start.2 = ((bf16[32,32,256]{2,1,0:T(8,128)(2,1)}), bf16[32,32,256]{2,1,0:T(8,128)(2,1)}, u32[]{:S(2)}, u32[]{:S(2)}) async-start(bf16[32,32,256]{2,1,0:T(8,128)(2,1)} %bitcast.185), calls=%async_computation.4 | async-start | bytes 1048576 | tf_op jit(solution)/shard_map/all_to_all | solution.py:202
  341.5 8.7 %all-to-all-start.3 = ((bf16[8,8,256]{2,1,0:T(8,128)(2,1)}), bf16[8,8,256]{2,1,0:T(8,128)(2,1)S(1)}, u32[]{:S(2)}, u32[]{:S(2)}) async-start(bf16[8,8,256]{2,1,0:T(8,128)(2,1)} %bitcast.163), calls=%async_computation.5 | async-start | bytes 65536 | tf_op jit(solution)/shard_map/all_to_all | solution.py:212
Sparse Core Ops, SparseCore 0:
  120.8 35.3 all-gather.8
  187.4 31.2 all-gather.4
  220.5 19.9 all-gather.6
  252.0 18.6 reduce-scatter.2
  273.1 33.5 reduce-scatter.4
